TPU v7x, 32 devices: a whole 2x2x4 slice. The times are simulated.
32 devices in a mesh: groups: 2 (over x), ctx: 4 (over y, core), head: 4 (over z).
Axes of the slice: x: 2, y: 2, z: 4, core: 2. Of those that a mesh axis runs over, the one named last changes fastest.
Arguments:
- tokens: bfloat16 [8192, 2048], P(('groups', 'ctx')), parts along dimension 0, may hold values from -30 to 30
- norm_one: float32 [2048], replicated, may hold values from 0.1 to 1.9
- w_qkv1: bfloat16 [2048, 3, 2048], P(None, None, 'head'), may hold values from -0.125 to 0.125
- lin_gain: float32 [2048], P('head'), may hold values from 0.1 to 1.9
- w_out1: bfloat16 [2048, 2048], P('head'), may hold values from -0.125 to 0.125
- norm_two: float32 [2048], replicated, may hold values from 0.1 to 1.9
- w_qkv2: bfloat16 [2048, 3, 2048], P(None, None, 'head'), may hold values from -0.125 to 0.125
- q_gain: float32 [128], replicated, may hold values from 0.4 to 2.5
- k_gain: float32 [128], replicated, may hold values from 0.4 to 2.5
- w_out2: bfloat16 [2048, 2048], P('head'), may hold values from -0.125 to 0.125
- neighbours: int32 [16, 8], P('ctx'), may hold values from -1 to 15, as said below
Outputs:
- mixed: bfloat16 [8192, 2048], P(('groups', 'ctx', 'head')), parts along dimension 0
There are 2 independent parts, one for each index of `groups`. A program takes and returns all parts, laid end to end along the dimension named above; an argument that names none is the same for every part. Nothing has to cross between parts.
Inputs may be any that keep to these rules, and one draw needn't show every extreme that they name: `neighbours`: tile (i, j, l) of the 4 x 2 x 2 grid is number (i * 2 + j) * 2 + l, and its tokens are a whole tile of the stream. Entry 0 of row t is t itself; every other entry is -1 or a tile other than t whose grid position differs from t's by at most one in each dimension; the tiles of one row are distinct.
All inputs are finite; a program needn't handle non-finite values.
Results may differ from a plain program's by a relative error of at most 0.013.
Values may be sent and summed in bfloat16 or wider, within the bound.
No kernel may reach another device: no remote copies, remote signals or barrier semaphores. Data moves between devices by JAX's collectives and lax.ppermute only.
A program may use at most 192 MiB of HBM per device.

v0:
```python
import math
import jax
import jax.numpy as jnp
from jax import lax
from jax.sharding import PartitionSpec as P

TILE = 256
GY = 2
GZ = 2
EPS = 1e-06


def with_halo(shard, sides, width):
    for axis, dim in sides:
        size, length = (lax.axis_size(axis), shard.shape[dim])
        up = [(i, (i + 1) % size) for i in range(size - 1)]
        down = [(j, i) for i, j in up]
        last = lax.slice_in_dim(shard, length - width, length, axis=dim)
        first = lax.slice_in_dim(shard, 0, width, axis=dim)
        before = lax.ppermute(last, axis, up)
        after = lax.ppermute(first, axis, down)
        shard = jnp.concatenate([before, shard, after], axis=dim)
    return shard


def rms_rows(value, gain):
    mean_sq = jnp.mean(value * value, axis=-1, keepdims=True)
    return value * lax.rsqrt(mean_sq + EPS) * gain


def feature_map(value):
    return jnp.where(value > 0, value + 1.0, jnp.exp(jnp.minimum(value, 0.0)))


def split_two(value):
    high_part = value.astype(jnp.bfloat16)
    low_part = (value - high_part.astype(jnp.float32)).astype(jnp.bfloat16)
    return (high_part, low_part)


def on_device(
    tokens, norm_one, w_qkv1, lin_gain, w_out1, norm_two, w_qkv2, q_gain, k_gain, w_out2, neighbours
):
    f32, bf16 = (jnp.float32, jnp.bfloat16)
    tok_rows, feature_width = tokens.shape
    inner_dev = w_qkv1.shape[2]
    head_dim = q_gain.shape[0]
    heads_dev = inner_dev // head_dim
    block_rows = 2 * TILE
    block_count = tok_rows // block_rows
    rows_mine = tok_rows // lax.axis_size("head")
    head_index = lax.axis_index("head")
    ctx_index = lax.axis_index("ctx")
    ctx_size = lax.axis_size("ctx")
    normed = rms_rows(tokens.astype(f32), norm_one).astype(bf16)
    projected = jnp.dot(
        normed, w_qkv1.reshape(feature_width, 3 * inner_dev), preferred_element_type=f32
    )
    projected = projected.reshape(tok_rows, 3, heads_dev, head_dim)
    query_map = feature_map(projected[:, 0]).astype(bf16)
    key_map = feature_map(projected[:, 1]).astype(bf16)
    value_one = projected[:, 2].astype(bf16)
    q_blocks = query_map.reshape(block_count, block_rows, heads_dev, head_dim)
    k_blocks = key_map.reshape(block_count, block_rows, heads_dev, head_dim)
    v_blocks = value_one.reshape(block_count, block_rows, heads_dev, head_dim)
    block_states = jnp.einsum("nthe,nthf->nhef", k_blocks, v_blocks, preferred_element_type=f32)
    own_total = jnp.sum(block_states, axis=0)
    all_totals = lax.all_gather(own_total.astype(bf16), "ctx", axis=0).astype(f32)
    earlier_dev = jnp.arange(ctx_size, dtype=jnp.int32) < ctx_index
    carried = jnp.sum(jnp.where(earlier_dev[:, None, None, None], all_totals, 0.0), axis=0)
    causal = lax.broadcasted_iota(jnp.int32, (block_rows, block_rows), 0) >= lax.broadcasted_iota(
        jnp.int32, (block_rows, block_rows), 1
    )
    w_qkv2_flat = w_qkv2.reshape(feature_width, 3 * inner_dev)
    residual_parts = []
    q_parts, k_parts, v_parts = ([], [], [])
    previous = None
    for n in range(block_count):
        q_n, k_n, v_n = (q_blocks[n], k_blocks[n], v_blocks[n])
        scores = jnp.einsum("the,she->hts", q_n, k_n, preferred_element_type=f32)
        scores = jnp.where(causal, scores, 0.0)
        score_high, score_low = split_two(scores)
        within = jnp.einsum("hts,she->the", score_high, v_n, preferred_element_type=f32)
        within = within + jnp.einsum("hts,she->the", score_low, v_n, preferred_element_type=f32)
        state_high, state_low = split_two(carried)
        carried_term = jnp.einsum("the,hef->thf", q_n, state_high, preferred_element_type=f32)
        carried_term = carried_term + jnp.einsum(
            "the,hef->thf", q_n, state_low, preferred_element_type=f32
        )
        carried = carried + block_states[n]
        combined = within + carried_term
        attn_n = (
            rms_rows(combined, lin_gain.reshape(heads_dev, head_dim))
            .astype(bf16)
            .reshape(block_rows, inner_dev)
        )
        partial = jnp.dot(attn_n, w_out1, preferred_element_type=f32).astype(bf16)
        if previous is not None:
            partial, previous = lax.optimization_barrier((partial, previous))
            residual_parts[-1] = previous
        summed = lax.psum(partial, "head").astype(f32)
        tokens_n = tokens[n * block_rows : (n + 1) * block_rows].astype(f32)
        residual_n = (tokens_n + summed).astype(bf16)
        residual_parts.append(residual_n)
        previous = residual_n
        normed_n = rms_rows(residual_n.astype(f32), norm_two).astype(bf16)
        proj_n = jnp.dot(normed_n, w_qkv2_flat, preferred_element_type=f32)
        proj_n = proj_n.reshape(block_rows, 3, heads_dev, head_dim)
        q_parts.append(rms_rows(proj_n[:, 0], q_gain).astype(bf16))
        k_parts.append(rms_rows(proj_n[:, 1], k_gain).astype(bf16))
        v_parts.append(proj_n[:, 2].astype(bf16))
    residual = jnp.concatenate(residual_parts, axis=0)
    query_hat = jnp.concatenate(q_parts, axis=0)
    key_hat = jnp.concatenate(k_parts, axis=0)
    value_two = jnp.concatenate(v_parts, axis=0)
    key_value = jnp.stack([key_hat, value_two], axis=1).reshape(tok_rows, 2 * inner_dev)
    plane_tiles = GY * GZ
    widened = with_halo(key_value, (("ctx", 0),), plane_tiles * TILE)
    buffer_rows = widened.shape[0]
    buffer_tiles = buffer_rows // TILE
    tile_count = tok_rows // TILE
    base_tile = ctx_index * tile_count - plane_tiles
    widened = widened.reshape(buffer_rows, 2, heads_dev, head_dim)
    buffer_ids = base_tile + jnp.arange(buffer_tiles, dtype=jnp.int32)
    valid = jnp.any(
        (neighbours[:, :, None] == buffer_ids[None, None, :]) & (neighbours[:, :, None] >= 0),
        axis=1,
    )
    valid_keys = jnp.repeat(valid, TILE, axis=1)
    query_tiles = query_hat.reshape(tile_count, TILE, heads_dev, head_dim)
    score_scale = 1.0 / math.sqrt(head_dim)
    tile_scores = (
        jnp.einsum("pthe,she->phts", query_tiles, widened[:, 0], preferred_element_type=f32)
        * score_scale
    )
    unnormed = jnp.where(valid_keys[:, None, None, :], jnp.exp(tile_scores), 0.0)
    weights = (unnormed / jnp.sum(unnormed, axis=-1, keepdims=True)).astype(bf16)
    attn_two = jnp.einsum("phts,she->pthe", weights, widened[:, 1], preferred_element_type=f32)
    attn_two = attn_two.astype(bf16).reshape(tok_rows, inner_dev)
    summed_two = lax.psum_scatter(
        jnp.dot(attn_two, w_out2, preferred_element_type=f32).astype(bf16),
        "head",
        scatter_dimension=0,
        tiled=True,
    ).astype(f32)
    residual_mine = lax.dynamic_slice_in_dim(residual, head_index * rows_mine, rows_mine, 0)
    return (residual_mine.astype(f32) + summed_two).astype(bf16)


def solution(mesh):
    in_specs = (
        P(("groups", "ctx"), None),
        P(),
        P(None, None, "head"),
        P("head"),
        P("head", None),
        P(),
        P(None, None, "head"),
        P(),
        P(),
        P("head", None),
        P("ctx", None),
    )
    out_specs = P(("groups", "ctx", "head"), None)
    return jax.shard_map(
        on_device, mesh=mesh, in_specs=in_specs, out_specs=out_specs, check_vma=False
    )
```

profile of v0, /device:TPU:0, one launch (start us, length us, event | category | flops | bytes accessed | tf_op | source)
XLA Modules:
  0.0 424.5 jit_solution(1946575152552089847)
XLA Ops:
  6.6 3.2 fusion.2
  9.9 8.8 %copy.60 = bf16[2048,3,512]{0,2,1:T(8,128)(2,1)} copy(bf16[2048,3,512]{2,0,1:T(8,128)(2,1)} %param.13) | data formatting | bytes 12582912 | tf_op args[2]
  18.7 10.3 %fusion.12 = f32[1024,3,4,128]{3,0,2,1:T(8,128)S(1)} fusion(bf16[3,4,128,2048]{3,2,1,0:T(8,128)(2,1)} %bitcast.165, bf16[1024,2048]{1,0:T(8,128)(2,1)} %param.11, f32[2048]{0:T(1024)S(1)} %copy-done.15, f32[1024]{0:T(1024)S(1)} %add_rsqrt_fusion.6), kind=kOutput, calls=%fused_computation.21 | convolution fusion | flops 6450839552 | bytes 16789504 | tf_op jit(solution)/shard_map/dot_general | solution.py:56
  29.0 1.1 slice.199
  30.1 1.0 select_convert_fusion.4
  31.1 2.6 fusion.56
  33.7 2.7 fusion.57
  36.4 2.0 fusion.73
  38.5 8.8 %all-gather = bf16[16,128,128]{2,1,0:T(8,128)(2,1)S(1)} all-gather(bf16[4,128,128]{2,1,0:T(8,128)(2,1)S(1)} %get-tuple-element.27), channel_id=2, replica_groups=mesh['groups'=2,'ctx'=4,'head'=4] {'ctx'}, dimensions={0}, use_global_device_ids=true | all-gather | bytes 655360 | tf_op jit(solution)/shard_map/all_gather | solution.py:68
  47.5 0.3 fusion.59
  47.8 0.3 convolution_add_fusion
  48.2 0.4 fusion.58
  48.6 0.4 convolution_add_fusion.1
  48.9 1.1 copy-done.3
  50.0 0.3 copy-done.4
  50.3 0.9 fusion.18
  51.2 0.6 copy-done.2
  51.8 0.9 fusion.17
  52.7 1.1 multiply_reduce_fusion.4
  53.8 1.1 multiply_reduce_fusion.5
  55.2 2.6 convolution_convert_fusion.1
  57.8 2.6 convolution_convert_fusion.2
  60.4 84.9 %all-reduce.3.cloned.1.call-done = bf16[512,2048]{1,0:T(8,128)(2,1)} async-done(((bf16[512,2048]{1,0:T(8,128)(2,1)}), bf16[512,2048]{1,0:T(8,128)(2,1)}) %all-reduce.3.cloned.1.call-update) | async-done | bytes 2097168 | tf_op jit(solution)/shard_map/psum | solution.py:101
  145.3 3.2 fusion.5
  148.8 9.3 %copy.71 = bf16[2048,3,512]{0,2,1:T(8,128)(2,1)} copy(bf16[2048,3,512]{2,0,1:T(8,128)(2,1)} %param.17) | data formatting | bytes 12582912 | tf_op args[6]
  158.1 5.7 %fusion.25 = f32[512,3,4,128]{3,0,2,1:T(8,128)S(1)} fusion(bf16[3,4,128,2048]{3,2,1,0:T(8,128)(2,1)} %bitcast.163, bf16[512,2048]{1,0:T(8,128)(2,1)S(1)} %get-tuple-element.7, f32[2048]{0:T(1024)S(1)} %copy-done.16, f32[512]{0:T(512)S(1)} %add_rsqrt_fusion.8), kind=kOutput, calls=%fused_computation.45 | convolution fusion | flops 3225419776 | bytes 11544576 | tf_op jit(solution)/shard_map/dot_general | solution.py:107
  163.9 0.6 multiply_reduce_fusion.3
  164.5 1.0 copy-done.7
  165.6 68.5 %all-reduce.5.cloned.1.call-done = bf16[512,2048]{1,0:T(8,128)(2,1)} async-done(((bf16[512,2048]{1,0:T(8,128)(2,1)}), bf16[512,2048]{1,0:T(8,128)(2,1)}) %all-reduce.5.cloned.1.call-update) | async-done | bytes 2097168 | tf_op jit(solution)/shard_map/psum | solution.py:101
  234.1 3.2 fusion.8
  237.4 6.5 %fusion.22 = f32[512,3,4,128]{3,0,2,1:T(8,128)S(1)} fusion(bf16[3,4,128,2048]{3,2,1,0:T(8,128)(2,1)} %bitcast.164, bf16[512,2048]{1,0:T(8,128)(2,1)S(1)} %get-tuple-element.16, f32[512]{0:T(512)S(1)} %add_rsqrt_fusion.7, f32[2048]{0:T(1024)S(1)} %copy-done.16), kind=kOutput, calls=%fused_computation.43 | convolution fusion | flops 3225419776 | bytes 11544576 | tf_op jit(solution)/shard_map/dot_general | solution.py:107
  243.9 0.6 multiply_reduce_fusion.2
  244.7 1.0 copy-done.8
  245.8 1.4 multiply_convert_fusion.2
  247.3 1.5 pad_maximum_fusion.1
  248.7 4.0 copy.72
  252.7 1.3 collective-permute-start.1
  254.0 4.4 %collective-permute-start = (bf16[1024,1024]{0,1:T(8,128)(2,1)}, bf16[1024,1024]{0,1:T(8,128)(2,1)}, u32[]{:S(2)}, u32[]{:S(2)}) collective-permute-start(bf16[1024,1024]{0,1:T(8,128)(2,1)} %bitcast.169), channel_id=1, source_target_pairs={{0,4},{4,8},{8,12},{1,5},{5,9},{9,13},{2,6},{6,10},{10,14},{3,7},{... | collective-permute-start | bytes 6291464 | tf_op jit(solution)/shard_map/ppermute | solution.py:20
  258.6 1.0 pad_maximum_fusion.2
  259.6 3.9 copy.74
  263.6 4.0 copy.73
  267.5 3.1 pad_maximum_fusion
  270.7 19.7 %fusion = (f32[4,4,256]{2,0,1:T(4,128)S(1)}, f32[4,3072,4,256]{3,1,2,0:T(8,128)}) fusion(pred[4,3072]{1,0:T(4,128)(4,1)S(1)} %bitcast.174, bf16[4,256,4,128]{3,1,0,2:T(8,128)(2,1)S(1)} %bitcast.170, bf16[3072,2,4,128]{3,0,2,1:T(8,128)(2,1)S(1)} %pad_maximum_fusion), kind=kOutput, calls=%fused_computation.2 | convolution fusion | flops 3258970112 | bytes 54554624 | tf_op jit(solution)/shard_map/pthe,she->phts/dot_general | solution.py:133
  290.3 22.4 %fusion.40 = bf16[4,256,4,128]{1,3,0,2:T(8,128)(2,1)S(1)} fusion(f32[4,3072,4,256]{3,1,2,0:T(8,128)} %get-tuple-element.34, f32[4,4,256]{2,0,1:T(4,128)S(1)} %get-tuple-element.33, pred[4,3072]{1,0:T(4,128)(4,1)S(1)} %bitcast.175, bf16[3072,2,4,128]{3,0,2,1:T(8,128)(2,1)S(1)} %pad_maximum_fusion), kind=kOutput, calls=%fused_computation.64 | convolution fusion | flops 3272081408 | bytes 54554624 | tf_op jit(solution)/shard_map/phts,she->pthe/dot_general | solution.py:138
  312.7 0.7 copy.77
  313.4 5.9 %convolution_convert_fusion = bf16[1024,2048]{1,0:T(8,128)(2,1)} fusion(bf16[512,2048]{1,0:T(8,128)(2,1)} %param.20, bf16[128,8,4,128]{3,2,1,0:T(4,128)(2,1)S(1)} %bitcast.171), kind=kOutput, calls=%fused_computation.32 | convolution fusion | flops 2149580800 | bytes 7340032 | tf_op jit(solution)/shard_map/dot_general | solution.py:141
  319.3 95.4 %reduce-scatter.2.cloned.1.call-done = bf16[256,2048]{1,0:T(8,128)(2,1)} async-done(((bf16[1024,2048]{1,0:T(8,128)(2,1)}), bf16[256,2048]{1,0:T(8,128)(2,1)}) %reduce-scatter.2.cloned.1.call-update) | async-done | bytes 1048592 | tf_op jit(solution)/shard_map/reduce_scatter | solution.py:140
  414.7 3.3 add_convert_fusion.2
  (58 shorter events, 1.5 us)
Async XLA Ops:
  6.5 48.6 %copy-start = (bf16[512,2048]{1,0:T(8,128)(2,1)S(1)}, bf16[512,2048]{1,0:T(8,128)(2,1)}, u32[]{:S(2)}) copy-start(bf16[512,2048]{1,0:T(8,128)(2,1)} %param.15) | copy-start | bytes 6291460
  6.5 138.7 %all-reduce.3.cloned.1.call-start = ((), (), s32[]{:S(2)}) async-start(), calls=%async_computation.1 | async-start | bytes 4194304 | tf_op jit(solution)/shard_map/psum | solution.py:101
  9.8 8.9 %copy-start.15 = (f32[2048]{0:T(1024)S(1)}, f32[2048]{0:T(1024)}, u32[]{:S(2)}) copy-start(f32[2048]{0:T(1024)} %param.12) | copy-start | bytes 24580
  31.1 2.7 copy-start.9
  47.8 2.2 copy-start.3
  47.8 2.5 copy-start.4
  48.5 3.2 copy-start.2
  53.8 1.1 copy-start.12
  57.8 176.4 %all-reduce.5.cloned.1.call-start = ((), (), s32[]{:S(2)}) async-start(), calls=%async_computation.2 | async-start | bytes 4194304 | tf_op jit(solution)/shard_map/psum | solution.py:101
  148.5 9.6 %copy-start.5 = (bf16[512,2048]{1,0:T(8,128)(2,1)}, bf16[512,2048]{1,0:T(8,128)(2,1)S(1)}, u32[]{:S(2)}) copy-start(bf16[512,2048]{1,0:T(8,128)(2,1)S(1)} %get-tuple-element.7) | copy-start | bytes 6291460
  148.5 9.6 %copy-start.16 = (f32[2048]{0:T(1024)S(1)}, f32[2048]{0:T(1024)}, u32[]{:S(2)}) copy-start(f32[2048]{0:T(1024)} %param.16) | copy-start | bytes 24580
  148.5 266.2 %reduce-scatter.2.cloned.1.call-start = ((), (), s32[]{:S(2)}) async-start(), calls=%async_computation.3 | async-start | bytes 5242880 | tf_op jit(solution)/shard_map/reduce_scatter | solution.py:140
  163.9 1.7 copy-start.7
  237.3 6.5 %copy-start.6 = (bf16[512,2048]{1,0:T(8,128)(2,1)}, bf16[512,2048]{1,0:T(8,128)(2,1)S(1)}, u32[]{:S(2)}) copy-start(bf16[512,2048]{1,0:T(8,128)(2,1)S(1)} %get-tuple-element.16) | copy-start | bytes 6291460
  243.9 1.9 copy-start.8
  243.9 1.9 copy-start.13
  243.9 1.9 copy-start.14
  247.2 11.1 %copy-start.11 = (s32[4,8]{1,0:T(4,128)S(1)}, s32[4,8]{1,0:T(4,128)}, u32[]{:S(2)}) copy-start(s32[4,8]{1,0:T(4,128)} %param.21) | copy-start | bytes 388
  252.7 6.9 %collective-permute-start.1 = (bf16[1024,1024]{0,1:T(8,128)(2,1)}, bf16[1024,1024]{0,1:T(8,128)(2,1)}, u32[]{:S(2)}, u32[]{:S(2)}) collective-permute-start(bf16[1024,1024]{0,1:T(8,128)(2,1)} %bitcast.168), channel_id=1, source_target_pairs={{4,0},{8,4},{12,8},{5,1},{9,5},{13,9},{6,2},{10,6},{14,10},{7,3},{... | collective-permute-start | bytes 6291464 | tf_op jit(solution)/shard_map/ppermute | solution.py:21
  254.0 9.6 %collective-permute-start = (bf16[1024,1024]{0,1:T(8,128)(2,1)}, bf16[1024,1024]{0,1:T(8,128)(2,1)}, u32[]{:S(2)}, u32[]{:S(2)}) collective-permute-start(bf16[1024,1024]{0,1:T(8,128)(2,1)} %bitcast.169), channel_id=1, source_target_pairs={{0,4},{4,8},{8,12},{1,5},{5,9},{9,13},{2,6},{6,10},{10,14},{3,7},{... | collective-permute-start | bytes 6291464 | tf_op jit(solution)/shard_map/ppermute | solution.py:20
  267.5 3.1 copy-start.10
  319.3 98.7 %copy-start.1 = (bf16[512,2048]{1,0:T(8,128)(2,1)S(1)}, bf16[512,2048]{1,0:T(8,128)(2,1)}, u32[]{:S(2)}) copy-start(bf16[512,2048]{1,0:T(8,128)(2,1)} %param.15) | copy-start | bytes 6291460
Sparse Core Ops, SparseCore 0:
  57.9 87.3 all-reduce.2
  148.6 85.4 all-reduce.4
  319.4 95.2 reduce-scatter.1
where the time goes:
time: 426 us; the launch traced here: 425 us
  waiting for transfers between devices  249 us (58%)
  matrix products  88.3 us (21%)
  local copies, waits for them, and re-layouts  36.2 us (8%)
  other arithmetic  23 us (5%)
  between operations  13.5 us (3%)
  blocking collectives  8.83 us (2%)
  starting transfers between devices  5.96 us (1%)
    psum x2, waiting for transfers between devices, on_device(): summed = lax.psum(partial, 'head').astype(f32)  153 us
    reduce_scatter x1, waiting for transfers between devices, on_device(): lax.psum_scatter(jnp.dot(attn_two, w_out2, preferred_element_type=f32).as...  95.4 us
    dot_general x1, matrix products, on_device(): jnp.einsum('phts,she->pthe', weights, widened[:, 1], preferred_element_ty...  22.4 us
    unnamed x38, local copies, waits for them, and re-layouts  22.4 us
    dot_general x1, matrix products, on_device(): jnp.einsum('pthe,she->phts', query_tiles, widened[:, 0], preferred_elemen...  19.7 us
    dot_general x2, matrix products, on_device(): proj_n = jnp.dot(normed_n, w_qkv2_flat, preferred_element_type=f32)  12.2 us
    reduce_sum x5, other arithmetic, rms_rows(): mean_sq = jnp.mean(value * value, axis=-1, keepdims=True)  10.8 us
    dot_general x1, matrix products, on_device(): jnp.dot(normed, w_qkv1.reshape(feature_width, 3 * inner_dev), preferred_e...  10.3 us
  transfers between devices with their start and end apart: 5, of which 3 were waited for; matrix products, arithmetic and copies ran while one was open for 6% of the time, Pallas kernels for 0%

commit v1 on v0

--- a/solution.py
+++ b/solution.py
@@ -1,3 +1,4 @@
+import functools
 import math
 import jax
 import jax.numpy as jnp
@@ -8,6 +9,13 @@
 GY = 2
 GZ = 2
 EPS = 1e-06
+
+
+def lead_trails(vector, axis_key):
+    return lax.all_gather(vector, axis_name=axis_key).sum(axis=0)
+
+
+post_positions = functools.partial(lead_trails, axis_key="head")
 
 
 def with_halo(shard, sides, width):
@@ -98,7 +106,7 @@
         if previous is not None:
             partial, previous = lax.optimization_barrier((partial, previous))
             residual_parts[-1] = previous
-        summed = lax.psum(partial, "head").astype(f32)
+        summed = post_positions(partial).astype(f32)
         tokens_n = tokens[n * block_rows : (n + 1) * block_rows].astype(f32)
         residual_n = (tokens_n + summed).astype(bf16)
         residual_parts.append(residual_n)

time: 426 us -> 565 us (1.33)
  waiting for transfers between devices: 249 us -> 373 us
  other arithmetic: 23 us -> 37.5 us
    all_gather x0 -> x2, waiting for transfers between devices: none -> 278 us  [lead_trails(): return lax.all_gather(vector, axis_name=axis_key).sum(axis=0)]
    psum x2 -> x0, waiting for transfers between devices: 153 us -> none  [on_device(): summed = lax.psum(partial, 'head').astype(f32)]
    reduce_sum x0 -> x2, other arithmetic: none -> 14.5 us  [lead_trails(): return lax.all_gather(vector, axis_name=axis_key).sum(axis=0)]
  transfers between devices with their start and end apart: 5 -> 5, of which waited for: 3 -> 3; matrix products, arithmetic and copies ran while one was open for 6% -> 4% of each run, Pallas kernels for 0% -> 0%
where the time goes in v1:
time: 565 us; the launch traced here: 564 us
  waiting for transfers between devices  373 us (66%)
  matrix products  88.7 us (16%)
  other arithmetic  37.5 us (7%)
  local copies, waits for them, and re-layouts  36.3 us (6%)
  between operations  13.5 us (2%)
  blocking collectives  8.83 us (2%)
  starting transfers between devices  5.96 us (1%)
    all_gather x2, waiting for transfers between devices, lead_trails(): return lax.all_gather(vector, axis_name=axis_key).sum(axis=0)  278 us
    reduce_scatter x1, waiting for transfers between devices, on_device(): lax.psum_scatter(jnp.dot(attn_two, w_out2, preferred_element_type=f32).as...  94.6 us
    unnamed x38, local copies, waits for them, and re-layouts  22.4 us
    dot_general x1, matrix products, on_device(): jnp.einsum('phts,she->pthe', weights, widened[:, 1], preferred_element_ty...  22.4 us
    dot_general x1, matrix products, on_device(): jnp.einsum('pthe,she->phts', query_tiles, widened[:, 0], preferred_elemen...  19.7 us
    reduce_sum x2, other arithmetic, lead_trails(): return lax.all_gather(vector, axis_name=axis_key).sum(axis=0)  14.5 us
    dot_general x2, matrix products, on_device(): proj_n = jnp.dot(normed_n, w_qkv2_flat, preferred_element_type=f32)  12.5 us
  transfers between devices with their start and end apart: 5, of which 3 were waited for; matrix products, arithmetic and copies ran while one was open for 4% of the time, Pallas kernels for 0%

profile of v1, /device:TPU:0, one launch (start us, length us, event | category | flops | bytes accessed | tf_op | source)
XLA Modules:
  0.0 563.9 jit_solution(10015666180170650274)
XLA Ops:
  6.6 3.2 fusion.2
  9.9 8.8 %copy.60 = bf16[2048,3,512]{0,2,1:T(8,128)(2,1)} copy(bf16[2048,3,512]{2,0,1:T(8,128)(2,1)} %param.13) | data formatting | bytes 12582912 | tf_op args[2]
  18.7 10.3 %fusion.12 = f32[1024,3,4,128]{3,0,2,1:T(8,128)S(1)} fusion(bf16[3,4,128,2048]{3,2,1,0:T(8,128)(2,1)} %bitcast.169, bf16[1024,2048]{1,0:T(8,128)(2,1)} %param.11, f32[2048]{0:T(1024)S(1)} %copy-done.15, f32[1024]{0:T(1024)S(1)} %add_rsqrt_fusion.6), kind=kOutput, calls=%fused_computation.21 | convolution fusion | flops 6450839552 | bytes 16789504 | tf_op jit(solution)/shard_map/dot_general | solution.py:64
  29.0 1.1 slice.199
  30.1 1.0 select_convert_fusion.4
  31.1 2.6 fusion.56
  33.7 2.7 fusion.57
  36.4 2.0 fusion.73
  38.5 8.8 %all-gather = bf16[16,128,128]{2,1,0:T(8,128)(2,1)S(1)} all-gather(bf16[4,128,128]{2,1,0:T(8,128)(2,1)S(1)} %get-tuple-element.27), channel_id=2, replica_groups=mesh['groups'=2,'ctx'=4,'head'=4] {'ctx'}, dimensions={0}, use_global_device_ids=true | all-gather | bytes 655360 | tf_op jit(solution)/shard_map/all_gather | solution.py:76
  47.8 0.3 convolution_add_fusion
  48.2 0.4 fusion.58
  48.6 0.4 convolution_add_fusion.1
  48.9 1.1 copy-done.3
  50.3 0.9 fusion.18
  51.2 0.6 copy-done.2
  51.8 0.9 fusion.17
  52.7 1.1 multiply_reduce_fusion.4
  53.8 1.1 multiply_reduce_fusion.5
  55.2 2.7 convolution_convert_fusion.1
  57.9 2.6 convolution_convert_fusion.2
  60.5 148.0 %all-gather.6.cloned.1.call-done = bf16[2048,2048]{1,0:T(8,128)(2,1)} async-done(((bf16[512,2048]{1,0:T(8,128)(2,1)}), bf16[2048,2048]{1,0:T(8,128)(2,1)}) %all-gather.6.cloned.1.call-update) | async-done | bytes 8388624 | tf_op jit(solution)/shard_map/all_gather | solution.py:15
  208.5 7.3 %reduce_sum.137 = bf16[512,2048]{1,0:T(8,128)(2,1)} reduce(bf16[4,512,2048]{2,1,0:T(8,128)(2,1)} %bitcast.166, bf16[]{:T(256)} %constant.40.clone.1), dimensions={0}, to_apply=%region_5.6 | reduce | flops 3145728 | bytes 10485762 | tf_op jit(solution)/shard_map/reduce_sum | solution.py:15
  215.8 3.2 fusion.5
  219.3 9.5 %copy.71 = bf16[2048,3,512]{0,2,1:T(8,128)(2,1)} copy(bf16[2048,3,512]{2,0,1:T(8,128)(2,1)} %param.17) | data formatting | bytes 12582912 | tf_op args[6]
  228.8 6.0 %fusion.25 = f32[512,3,4,128]{3,0,2,1:T(8,128)S(1)} fusion(bf16[3,4,128,2048]{3,2,1,0:T(8,128)(2,1)} %bitcast.167, bf16[512,2048]{1,0:T(8,128)(2,1)S(1)} %get-tuple-element.7, f32[2048]{0:T(1024)S(1)} %copy-done.16, f32[512]{0:T(512)S(1)} %add_rsqrt_fusion.8), kind=kOutput, calls=%fused_computation.45 | convolution fusion | flops 3225419776 | bytes 11544576 | tf_op jit(solution)/shard_map/dot_general | solution.py:115
  234.8 0.6 multiply_reduce_fusion.3
  235.5 1.0 copy-done.7
  236.5 130.5 %all-gather.8.cloned.1.call-done = bf16[2048,2048]{1,0:T(8,128)(2,1)} async-done(((bf16[512,2048]{1,0:T(8,128)(2,1)}), bf16[2048,2048]{1,0:T(8,128)(2,1)}) %all-gather.8.cloned.1.call-update) | async-done | bytes 8388624 | tf_op jit(solution)/shard_map/all_gather | solution.py:15
  367.0 7.2 %reduce_sum.138 = bf16[512,2048]{1,0:T(8,128)(2,1)} reduce(bf16[4,512,2048]{2,1,0:T(8,128)(2,1)} %bitcast.165, bf16[]{:T(256)} %constant.40.clone.1), dimensions={0}, to_apply=%region_6.7 | reduce | flops 3145728 | bytes 10485762 | tf_op jit(solution)/shard_map/reduce_sum | solution.py:15
  374.2 3.2 fusion.8
  377.5 6.5 %fusion.22 = f32[512,3,4,128]{3,0,2,1:T(8,128)S(1)} fusion(bf16[3,4,128,2048]{3,2,1,0:T(8,128)(2,1)} %bitcast.168, bf16[512,2048]{1,0:T(8,128)(2,1)S(1)} %get-tuple-element.16, f32[512]{0:T(512)S(1)} %add_rsqrt_fusion.7, f32[2048]{0:T(1024)S(1)} %copy-done.16), kind=kOutput, calls=%fused_computation.43 | convolution fusion | flops 3225419776 | bytes 11544576 | tf_op jit(solution)/shard_map/dot_general | solution.py:115
  384.0 0.6 multiply_reduce_fusion.2
  384.8 1.0 copy-done.8
  385.9 1.4 multiply_convert_fusion.2
  387.4 1.5 pad_maximum_fusion.1
  388.8 4.0 copy.72
  392.8 1.3 collective-permute-start.1
  394.1 4.4 collective-permute-start
  398.7 1.0 pad_maximum_fusion.2
  399.7 3.9 copy.74
  403.7 4.0 copy.73
  407.7 3.1 pad_maximum_fusion
  410.8 19.7 %fusion = (f32[4,4,256]{2,0,1:T(4,128)S(1)}, f32[4,3072,4,256]{3,1,2,0:T(8,128)}) fusion(pred[4,3072]{1,0:T(4,128)(4,1)S(1)} %bitcast.178, bf16[4,256,4,128]{3,1,0,2:T(8,128)(2,1)S(1)} %bitcast.174, bf16[3072,2,4,128]{3,0,2,1:T(8,128)(2,1)S(1)} %pad_maximum_fusion), kind=kOutput, calls=%fused_computation.2 | convolution fusion | flops 3258970112 | bytes 54554624 | tf_op jit(solution)/shard_map/pthe,she->phts/dot_general | solution.py:141
  430.4 22.4 %fusion.40 = bf16[4,256,4,128]{1,3,0,2:T(8,128)(2,1)S(1)} fusion(f32[4,3072,4,256]{3,1,2,0:T(8,128)} %get-tuple-element.34, f32[4,4,256]{2,0,1:T(4,128)S(1)} %get-tuple-element.33, pred[4,3072]{1,0:T(4,128)(4,1)S(1)} %bitcast.179, bf16[3072,2,4,128]{3,0,2,1:T(8,128)(2,1)S(1)} %pad_maximum_fusion), kind=kOutput, calls=%fused_computation.64 | convolution fusion | flops 3272081408 | bytes 54554624 | tf_op jit(solution)/shard_map/phts,she->pthe/dot_general | solution.py:146
  452.8 0.7 copy.77
  453.5 5.9 %convolution_convert_fusion = bf16[1024,2048]{1,0:T(8,128)(2,1)} fusion(bf16[512,2048]{1,0:T(8,128)(2,1)} %param.20, bf16[128,8,4,128]{3,2,1,0:T(4,128)(2,1)S(1)} %bitcast.175), kind=kOutput, calls=%fused_computation.32 | convolution fusion | flops 2149580800 | bytes 7340032 | tf_op jit(solution)/shard_map/dot_general | solution.py:149
  459.4 94.6 %reduce-scatter.2.cloned.1.call-done = bf16[256,2048]{1,0:T(8,128)(2,1)} async-done(((bf16[1024,2048]{1,0:T(8,128)(2,1)}), bf16[256,2048]{1,0:T(8,128)(2,1)}) %reduce-scatter.2.cloned.1.call-update) | async-done | bytes 1048592 | tf_op jit(solution)/shard_map/reduce_scatter | solution.py:148
  554.0 3.3 add_convert_fusion.2
  (60 shorter events, 2.1 us)
Async XLA Ops:
  6.5 48.6 %copy-start = (bf16[512,2048]{1,0:T(8,128)(2,1)S(1)}, bf16[512,2048]{1,0:T(8,128)(2,1)}, u32[]{:S(2)}) copy-start(bf16[512,2048]{1,0:T(8,128)(2,1)} %param.15) | copy-start | bytes 6291460
  6.5 202.0 %all-gather.6.cloned.1.call-start = ((), (), s32[]{:S(2)}) async-start(), calls=%async_computation.2 | async-start | bytes 10485760 | tf_op jit(solution)/shard_map/all_gather | solution.py:15
  9.8 8.9 %copy-start.15 = (f32[2048]{0:T(1024)S(1)}, f32[2048]{0:T(1024)}, u32[]{:S(2)}) copy-start(f32[2048]{0:T(1024)} %param.12) | copy-start | bytes 24580
  31.1 2.7 copy-start.9
  47.8 2.2 copy-start.3
  47.8 2.5 copy-start.4
  48.5 3.2 copy-start.2
  53.8 1.1 copy-start.12
  57.9 309.2 %all-gather.8.cloned.1.call-start = ((), (), s32[]{:S(2)}) async-start(), calls=%async_computation.3 | async-start | bytes 10485760 | tf_op jit(solution)/shard_map/all_gather | solution.py:15
  219.0 9.8 %copy-start.5 = (bf16[512,2048]{1,0:T(8,128)(2,1)}, bf16[512,2048]{1,0:T(8,128)(2,1)S(1)}, u32[]{:S(2)}) copy-start(bf16[512,2048]{1,0:T(8,128)(2,1)S(1)} %get-tuple-element.7) | copy-start | bytes 6291460
  219.0 9.8 %copy-start.16 = (f32[2048]{0:T(1024)S(1)}, f32[2048]{0:T(1024)}, u32[]{:S(2)}) copy-start(f32[2048]{0:T(1024)} %param.16) | copy-start | bytes 24580
  219.0 335.0 %reduce-scatter.2.cloned.1.call-start = ((), (), s32[]{:S(2)}) async-start(), calls=%async_computation.1 | async-start | bytes 5242880 | tf_op jit(solution)/shard_map/reduce_scatter | solution.py:148
  234.8 1.6 copy-start.7
  377.4 6.5 %copy-start.6 = (bf16[512,2048]{1,0:T(8,128)(2,1)}, bf16[512,2048]{1,0:T(8,128)(2,1)S(1)}, u32[]{:S(2)}) copy-start(bf16[512,2048]{1,0:T(8,128)(2,1)S(1)} %get-tuple-element.16) | copy-start | bytes 6291460
  384.0 1.9 copy-start.8
  384.0 1.9 copy-start.13
  384.0 1.9 copy-start.14
  387.3 11.1 %copy-start.11 = (s32[4,8]{1,0:T(4,128)S(1)}, s32[4,8]{1,0:T(4,128)}, u32[]{:S(2)}) copy-start(s32[4,8]{1,0:T(4,128)} %param.21) | copy-start | bytes 388
  392.8 6.9 %collective-permute-start.1 = (bf16[1024,1024]{0,1:T(8,128)(2,1)}, bf16[1024,1024]{0,1:T(8,128)(2,1)}, u32[]{:S(2)}, u32[]{:S(2)}) collective-permute-start(bf16[1024,1024]{0,1:T(8,128)(2,1)} %bitcast.172), channel_id=1, source_target_pairs={{4,0},{8,4},{12,8},{5,1},{9,5},{13,9},{6,2},{10,6},{14,10},{7,3},{... | collective-permute-start | bytes 6291464 | tf_op jit(solution)/shard_map/ppermute | solution.py:29
  394.1 9.6 %collective-permute-start = (bf16[1024,1024]{0,1:T(8,128)(2,1)}, bf16[1024,1024]{0,1:T(8,128)(2,1)}, u32[]{:S(2)}, u32[]{:S(2)}) collective-permute-start(bf16[1024,1024]{0,1:T(8,128)(2,1)} %bitcast.173), channel_id=1, source_target_pairs={{0,4},{4,8},{8,12},{1,5},{5,9},{9,13},{2,6},{6,10},{10,14},{3,7},{... | collective-permute-start | bytes 6291464 | tf_op jit(solution)/shard_map/ppermute | solution.py:28
  407.7 3.1 copy-start.10
  459.4 97.9 %copy-start.1 = (bf16[512,2048]{1,0:T(8,128)(2,1)S(1)}, bf16[512,2048]{1,0:T(8,128)(2,1)}, u32[]{:S(2)}) copy-start(bf16[512,2048]{1,0:T(8,128)(2,1)} %param.15) | copy-start | bytes 6291460
Sparse Core Ops, SparseCore 0:
  58.0 150.4 all-gather.5
  219.1 147.8 all-gather.7
  459.5 94.4 reduce-scatter.1
